TPU v7x, 256 devices: a whole 4x4x8 slice. The times are simulated.
256 devices in a mesh: dp: 32 (over z, x), et: 8 (over y, core).
Axes of the slice: x: 4, y: 4, z: 8, core: 2. Of those that a mesh axis runs over, the one named last changes fastest.
Arguments:
- tokens: bfloat16 [4096, 2048], P('dp', 'et'), may hold values from -6 to 6
- cotangent: bfloat16 [4096, 2048], P('dp', 'et'), may hold values from -1.5 to 1.5
- expert_ids: int32 [4096, 8], P('dp'), may hold values from 0 to 63, all different within a row; in each aligned block of 128 rows (0 to 127, 128 to 255, ...) at most 24 rows name the same one
- route_gates: bfloat16 [4096, 8], P('dp'), may hold values from 0.049804688 to 0.3984375
- gate_proj: bfloat16 [64, 2048, 1024], P('dp', None, 'et'), may hold values from -0.125 to 0.125
- up_proj: bfloat16 [64, 2048, 1024], P('dp', None, 'et'), may hold values from -0.125 to 0.125
- down_proj: bfloat16 [64, 1024, 2048], P('dp', 'et'), may hold values from -0.1875 to 0.1875
Outputs:
- mixed: bfloat16 [4096, 2048], P('dp', 'et')
- grad_tokens: bfloat16 [4096, 2048], P('dp', 'et')
- grad_gates: float32 [4096, 8], P('dp')
- grad_gate_proj: float32 [64, 2048, 1024], P('dp', None, 'et')
- grad_up_proj: float32 [64, 2048, 1024], P('dp', None, 'et')
- grad_down_proj: float32 [64, 1024, 2048], P('dp', 'et')
Inputs may be any that keep to these rules, and one draw needn't show every extreme that they name: `expert_ids`: each row names 8 different experts. Among the rows of one device (128 aligned rows), no expert is named more than 24 times, a bound that some block reaches.
All inputs are finite; a program needn't handle non-finite values.
Results may differ from a plain program's by a relative error of at most 0.015.
Values may be sent and summed in bfloat16 or wider, within the bound.
No kernel may reach another device: no remote copies, remote signals or barrier semaphores. Data moves between devices by JAX's collectives and lax.ppermute only.
A program may use at most 128 MiB of HBM per device.

v0:
```python
import jax
import jax.numpy as jnp
from jax import lax
from jax.sharding import PartitionSpec as P


def places_in_block(chosen, experts):
    flattened = chosen.reshape(-1)
    pairs = flattened.shape[0]
    onehot = (flattened[:, None] == jnp.arange(experts, dtype=jnp.int32)[None, :]).astype(
        jnp.bfloat16
    )
    rows = lax.broadcasted_iota(jnp.int32, (pairs, pairs), 0)
    cols = lax.broadcasted_iota(jnp.int32, (pairs, pairs), 1)
    earlier = (cols < rows).astype(jnp.bfloat16)
    before = jnp.dot(earlier, onehot, preferred_element_type=jnp.float32)
    return jnp.sum(before * onehot.astype(jnp.float32), axis=1).astype(jnp.int32)


def local(tokens, cotangent, expert_ids, route_gates, gate_proj, up_proj, down_proj):
    groups = lax.axis_size("dp")
    shards = lax.axis_size("et")
    local_experts, features, units = gate_proj.shape
    experts = local_experts * groups
    tok_rows, per_token = expert_ids.shape
    width = tokens.shape[1]
    capacity = 3 * tok_rows * per_token // (2 * experts)
    slots = experts * capacity
    places = places_in_block(expert_ids, experts)
    slot_index = (expert_ids.reshape(-1) * capacity + places).reshape(tok_rows, per_token)
    by_pair = slot_index.T
    match = by_pair[None, :, :] == jnp.arange(slots, dtype=jnp.int32)[:, None, None]
    select = jnp.any(match, axis=1).astype(jnp.bfloat16)
    gate_select = jnp.sum(
        jnp.where(match, route_gates.T[None, :, :].astype(jnp.float32), 0.0), axis=1
    ).astype(jnp.bfloat16)
    picked = jnp.dot(select, tokens, preferred_element_type=jnp.float32).astype(jnp.bfloat16)
    scaled = jnp.dot(gate_select, cotangent, preferred_element_type=jnp.float32).astype(
        jnp.bfloat16
    )
    routed = jnp.stack([picked, scaled]).reshape(2, experts, capacity, width)
    routed = lax.all_to_all(routed, "dp", split_axis=1, concat_axis=2, tiled=True)
    gathered = lax.all_gather(routed, "et", axis=0)
    expert_in = gathered[:, 0]
    expert_cot = gathered[:, 1]
    gate_w = gate_proj.reshape(local_experts, shards, width, units)
    up_w = up_proj.reshape(local_experts, shards, width, units)
    down_w = down_proj.reshape(local_experts, units, shards, width)
    pre_gate = jnp.einsum("jesd,ejdf->esf", expert_in, gate_w, preferred_element_type=jnp.float32)
    pre_up = jnp.einsum("jesd,ejdf->esf", expert_in, up_w, preferred_element_type=jnp.float32)
    sigmoid_gate = jax.nn.sigmoid(pre_gate)
    silu_gate = pre_gate * sigmoid_gate
    hidden = (silu_gate * pre_up).astype(jnp.bfloat16)
    out_part = jnp.einsum("esf,efd->esd", hidden, down_proj, preferred_element_type=jnp.float32)
    grad_hidden = jnp.einsum(
        "jesd,efjd->esf", expert_cot, down_w, preferred_element_type=jnp.float32
    )
    grad_pre_gate = (
        grad_hidden * pre_up * sigmoid_gate * (1.0 + pre_gate * (1.0 - sigmoid_gate))
    ).astype(jnp.bfloat16)
    grad_pre_up = (grad_hidden * silu_gate).astype(jnp.bfloat16)
    grad_down = jnp.einsum(
        "esf,jesd->efjd", hidden, expert_cot, preferred_element_type=jnp.float32
    ).reshape(local_experts, units, features)
    grad_gate_w = jnp.einsum(
        "jesd,esf->ejdf", expert_in, grad_pre_gate, preferred_element_type=jnp.float32
    ).reshape(local_experts, features, units)
    grad_up_w = jnp.einsum(
        "jesd,esf->ejdf", expert_in, grad_pre_up, preferred_element_type=jnp.float32
    ).reshape(local_experts, features, units)
    in_part = jnp.einsum(
        "esf,edf->esd", grad_pre_gate, gate_proj, preferred_element_type=jnp.float32
    )
    in_part = in_part + jnp.einsum(
        "esf,edf->esd", grad_pre_up, up_proj, preferred_element_type=jnp.float32
    )
    out_sum, in_sum = (
        lax.psum_scatter(out_part.astype(jnp.bfloat16), "et", scatter_dimension=2, tiled=True),
        lax.psum_scatter(in_part.astype(jnp.bfloat16), "et", scatter_dimension=2, tiled=True),
    )
    back_out, back_grad = (
        lax.all_to_all(out_sum, "dp", split_axis=1, concat_axis=0, tiled=True),
        lax.all_to_all(in_sum, "dp", split_axis=1, concat_axis=0, tiled=True),
    )
    back_out = back_out.reshape(slots, width)
    back_grad = back_grad.reshape(slots, width)
    mixed = jnp.einsum(
        "st,sd->td", gate_select, back_out, preferred_element_type=jnp.float32
    ).astype(jnp.bfloat16)
    grad_tokens = jnp.einsum(
        "st,sd->td", select, back_grad, preferred_element_type=jnp.float32
    ).astype(jnp.bfloat16)
    out_rows = (
        back_out[slot_index.reshape(-1)].reshape(tok_rows, per_token, width).astype(jnp.float32)
    )
    gate_part = jnp.sum(cotangent.astype(jnp.float32)[:, None, :] * out_rows, axis=2)
    grad_gates = lax.psum(gate_part, "et")
    return (mixed, grad_tokens, grad_gates, grad_gate_w, grad_up_w, grad_down)


def solution(mesh):
    in_specs = (
        P("dp", "et"),
        P("dp", "et"),
        P("dp", None),
        P("dp", None),
        P("dp", None, "et"),
        P("dp", None, "et"),
        P("dp", "et", None),
    )
    out_specs = (
        P("dp", "et"),
        P("dp", "et"),
        P("dp", None),
        P("dp", None, "et"),
        P("dp", None, "et"),
        P("dp", "et", None),
    )
    return jax.shard_map(local, mesh=mesh, in_specs=in_specs, out_specs=out_specs, check_vma=False)
```

profile of v0, /device:TPU:2, one launch (start us, length us, event | category | flops | bytes accessed | tf_op | source)
XLA Modules:
  0.0 328.7 jit_solution(484087539045145669)
XLA Ops:
  7.2 0.8 convert_bitcast_fusion
  8.0 0.8 copy.65
  9.6 5.6 %fusion = pred[1536,128]{1,0:T(8,128)(4,1)S(1)} fusion(s32[8,128]{1,0:T(8,128)S(1)} %copy.67), kind=kLoop, calls=%fused_computation.6 | loop fusion | flops 2949120 | bytes 200704 | tf_op jit(solution)/shard_map/reduce_or | solution.py:33
  15.2 8.1 %select_reduce_fusion = bf16[1536,128]{1,0:T(8,128)(2,1)S(1)} fusion(f32[8,128]{1,0:T(8,128)S(1)} %convert_bitcast_fusion, s32[8,128]{1,0:T(8,128)S(1)} %copy.67), kind=kLoop, calls=%fused_computation.4 | loop fusion | flops 4521984 | bytes 401408 | tf_op jit(solution)/shard_map/reduce_sum | solution.py:34
  23.4 1.2 convolution_convert_fusion.1
  24.6 1.3 convolution_convert_fusion.2
  26.1 50.7 %all_to_all.45 = bf16[2,64,24,256]{3,2,0,1:T(8,128)(2,1)S(1)} all-to-all(bf16[2,64,24,256]{3,2,0,1:T(8,128)(2,1)S(1)} %pad_maximum_fusion), channel_id=1, replica_groups=mesh['dp'=32,'et'=8] {'dp'}, dimensions={1} | all-to-all | bytes 3145728 | tf_op jit(solution)/shard_map/all_to_all | solution.py:42
  76.8 1.2 copy.70
  78.3 66.7 %all-gather.2.cloned.1.call-done = bf16[8,2,2,768,256]{4,3,0,2,1:T(8,128)(2,1)} async-done(((bf16[1,2,2,768,256]{4,3,0,2,1:T(8,128)(2,1)}), bf16[8,2,2,768,256]{4,3,0,2,1:T(8,128)(2,1)}) %all-gather.2.cloned.1.call-update) | async-done | bytes 12582928 | tf_op jit(solution)/shard_map/all_gather | solution.py:43
  145.0 4.7 %fusion.9 = f32[2,768,128]{2,1,0:T(8,128)S(1)} fusion(bf16[2,8,256,128]{3,2,1,0:T(8,128)(2,1)S(1)} %bitcast.108, bf16[8,2,2,768,256]{4,3,0,2,1:T(8,128)(2,1)} %all-gather.2.cloned.1.call-done), kind=kOutput, calls=%fused_computation.20 | convolution fusion | flops 805306368 | bytes 8126464 | tf_op jit(solution)/shard_map/jesd,ejdf->esf/dot_general | solution.py:50
  149.7 5.2 %fusion.8 = f32[2,768,128]{2,1,0:T(8,128)S(1)} fusion(bf16[2,8,256,128]{3,2,1,0:T(8,128)(2,1)S(1)} %bitcast.96, bf16[8,2,2,768,256]{4,3,0,2,1:T(8,128)(2,1)} %all-gather.2.cloned.1.call-done), kind=kOutput, calls=%fused_computation.19 | convolution fusion | flops 805306368 | bytes 8126464 | tf_op jit(solution)/shard_map/jesd,ejdf->esf/dot_general | solution.py:49
  154.9 2.0 multiply_convert_fusion
  157.0 0.7 copy-done.8
  157.7 4.4 %convolution_convert_fusion = bf16[2,768,2048]{2,1,0:T(8,128)(2,1)} fusion(bf16[2,768,128]{2,1,0:T(8,128)(2,1)S(1)} %get-tuple-element.32, bf16[2,128,2048]{2,1,0:T(8,128)(2,1)S(1)} %copy-done.10), kind=kOutput, calls=%fused_computation.9 | convolution fusion | flops 808452096 | bytes 7733248 | tf_op jit(solution)/shard_map/esf,efd->esd/dot_general | solution.py:54
  162.2 1.8 fusion.24
  164.0 4.4 %add_convert_fusion = bf16[2,768,2048]{2,1,0:T(8,128)(2,1)} fusion(f32[2,768,2048]{2,1,0:T(8,128)S(1)} %fusion.24, bf16[2,768,128]{2,1,0:T(8,128)(2,1)S(1)} %get-tuple-element.30, bf16[2,2048,128]{2,1,0:T(8,128)(2,1)S(1)} %copy-done.9), kind=kOutput, calls=%fused_computation.1 | convolution fusion | flops 811597824 | bytes 20316160 | tf_op jit(solution)/shard_map/esf,edf->esd/dot_general | solution.py:74
  168.4 39.3 %reduce-scatter.3.cloned.1.call-done = bf16[2,768,256]{2,1,0:T(8,128)(2,1)} async-done(((bf16[2,768,2048]{2,1,0:T(8,128)(2,1)}), bf16[2,768,256]{2,1,0:T(8,128)(2,1)}) %reduce-scatter.3.cloned.1.call-update) | async-done | bytes 786448 | tf_op jit(solution)/shard_map/reduce_scatter | solution.py:78
  207.7 2.8 copy.71
  210.5 10.1 %all-to-all-start.1 = ((bf16[2,768,256]{2,0,1:T(2,128)(2,1)}), bf16[2,768,256]{2,0,1:T(2,128)(2,1)S(1)}, u32[]{:S(2)}, u32[]{:S(2)}) async-start(bf16[2,768,256]{2,0,1:T(2,128)(2,1)} %copy.71), calls=%async_computation.2 | async-start | bytes 1572864 | tf_op jit(solution)/shard_map/all_to_all | solution.py:82
  221.5 33.8 %reduce-scatter.5.cloned.1.call-done = bf16[2,768,256]{2,1,0:T(8,128)(2,1)} async-done(((bf16[2,768,2048]{2,1,0:T(8,128)(2,1)}), bf16[2,768,256]{2,1,0:T(8,128)(2,1)}) %reduce-scatter.5.cloned.1.call-update) | async-done | bytes 786448 | tf_op jit(solution)/shard_map/reduce_scatter | solution.py:79
  255.3 2.9 copy.74
  258.2 10.1 %all-to-all-start.2 = ((bf16[2,768,256]{2,0,1:T(2,128)(2,1)}), bf16[2,768,256]{2,0,1:T(2,128)(2,1)}, u32[]{:S(2)}, u32[]{:S(2)}) async-start(bf16[2,768,256]{2,0,1:T(2,128)(2,1)} %copy.74), calls=%async_computation.4 | async-start | bytes 1572864 | tf_op jit(solution)/shard_map/all_to_all | solution.py:83
  268.3 5.5 %fusion.1 = f32[2,128,8,256]{1,3,2,0:T(8,128)S(1)} fusion(bf16[8,2,2,768,256]{4,3,0,2,1:T(8,128)(2,1)} %all-gather.2.cloned.1.call-done, bf16[2,768,128]{2,1,0:T(8,128)(2,1)} %copy-done.8), kind=kOutput, calls=%fused_computation.7 | convolution fusion | flops 805306368 | bytes 8781824 | tf_op jit(solution)/shard_map/esf,jesd->efjd/dot_general | solution.py:62
  273.8 1.8 copy.82
  275.6 6.7 %fusion.4 = f32[2,8,256,128]{3,2,1,0:T(8,128)} fusion(bf16[8,2,2,768,256]{4,3,0,2,1:T(8,128)(2,1)} %all-gather.2.cloned.1.call-done, bf16[2,768,128]{2,1,0:T(8,128)(2,1)} %copy-done.7), kind=kOutput, calls=%fused_computation.12 | convolution fusion | flops 805306368 | bytes 8781824 | tf_op jit(solution)/shard_map/jesd,esf->ejdf/dot_general | solution.py:68
  282.3 6.7 %fusion.5 = f32[2,8,256,128]{3,2,1,0:T(8,128)} fusion(bf16[8,2,2,768,256]{4,3,0,2,1:T(8,128)(2,1)} %all-gather.2.cloned.1.call-done, bf16[2,768,128]{2,1,0:T(8,128)(2,1)S(1)} %copy-done.6), kind=kOutput, calls=%fused_computation.13 | convolution fusion | flops 805306368 | bytes 8781824 | tf_op jit(solution)/shard_map/jesd,esf->ejdf/dot_general | solution.py:65
  289.2 3.9 %gather_fusion = bf16[1024,256]{1,0:T(8,128)(2,1)S(1)} fusion(bf16[1536,256]{1,0:T(8,128)(2,1)S(1)} %bitcast.97, s32[1024]{0:T(1024)S(1)} %broadcast_clamp_fusion), kind=kCustom, calls=%fused_computation | custom fusion | bytes 1052672 | tf_op jit(solution)/shard_map/gather | solution.py:94
  293.4 24.7 %psum.7 = f32[128,8]{1,0:T(8,128)S(1)} all-reduce(f32[128,8]{1,0:T(8,128)S(1)} %fusion.15), channel_id=1, replica_groups=mesh['dp'=32,'et'=8] {'et'}, use_global_device_ids=true, to_apply=%region_6.7 | all-reduce | flops 1024 | bytes 8192 | tf_op jit(solution)/shard_map/psum | solution.py:97
  318.1 0.7 copy.81
  318.8 1.0 convolution_convert_fusion.3
  319.7 1.2 copy.75
  321.1 1.1 convolution_convert_fusion.4
  (51 shorter events, 2.6 us)
Async XLA Ops:
  7.2 142.5 %copy-start = (bf16[2,2048,128]{2,1,0:T(8,128)(2,1)S(1)}, bf16[2,2048,128]{2,1,0:T(8,128)(2,1)}, u32[]{:S(2)}) copy-start(bf16[2,2048,128]{2,1,0:T(8,128)(2,1)} %param.11) | copy-start | bytes 3145732
  7.2 137.8 %all-gather.2.cloned.1.call-start = ((), (), s32[]{:S(2)}) async-start(), calls=%async_computation.5 | async-start | bytes 14155776 | tf_op jit(solution)/shard_map/all_gather | solution.py:43
  15.2 10.7 %copy-start.11 = (pred[1536,128]{1,0:T(8,128)(4,1)}, pred[1536,128]{1,0:T(8,128)(4,1)S(1)}, u32[]{:S(2)}) copy-start(pred[1536,128]{1,0:T(8,128)(4,1)S(1)} %fusion) | copy-start | bytes 589828
  24.6 120.4 %copy-start.9 = (bf16[2,2048,128]{2,1,0:T(8,128)(2,1)S(1)}, bf16[2,2048,128]{2,1,0:T(8,128)(2,1)}, u32[]{:S(2)}) copy-start(bf16[2,2048,128]{2,1,0:T(8,128)(2,1)} %param.12) | copy-start | bytes 3145732
  78.0 129.7 %reduce-scatter.3.cloned.1.call-start = ((), (), s32[]{:S(2)}) async-start(), calls=%async_computation.6 | async-start | bytes 7077888 | tf_op jit(solution)/shard_map/reduce_scatter | solution.py:78
  144.9 10.0 %copy-start.2 = (bf16[8,2,2,768,256]{4,3,0,2,1:T(8,128)(2,1)S(1)}, bf16[8,2,2,768,256]{4,3,0,2,1:T(8,128)(2,1)}, u32[]{:S(2)}) copy-start(bf16[8,2,2,768,256]{4,3,0,2,1:T(8,128)(2,1)} %all-gather.2.cloned.1.call-done) | copy-start | bytes 37748740
  149.7 5.3 %copy-start.10 = (bf16[2,128,2048]{2,1,0:T(8,128)(2,1)S(1)}, bf16[2,128,2048]{2,1,0:T(8,128)(2,1)}, u32[]{:S(2)}) copy-start(bf16[2,128,2048]{2,1,0:T(8,128)(2,1)} %param.13) | copy-start | bytes 3145732
  156.9 0.7 copy-start.8
  157.0 5.2 %copy-start.5 = (bf16[2,768,128]{2,1,0:T(8,128)(2,1)}, bf16[2,768,128]{2,1,0:T(8,128)(2,1)S(1)}, u32[]{:S(2)}) copy-start(bf16[2,768,128]{2,1,0:T(8,128)(2,1)S(1)} %get-tuple-element.31) | copy-start | bytes 1179652
  157.0 7.0 %copy-start.7 = (bf16[2,768,128]{2,1,0:T(8,128)(2,1)}, bf16[2,768,128]{2,1,0:T(8,128)(2,1)S(1)}, u32[]{:S(2)}) copy-start(bf16[2,768,128]{2,1,0:T(8,128)(2,1)S(1)} %get-tuple-element.30) | copy-start | bytes 1179652
  162.1 93.2 %reduce-scatter.5.cloned.1.call-start = ((), (), s32[]{:S(2)}) async-start(), calls=%async_computation.7 | async-start | bytes 7077888 | tf_op jit(solution)/shard_map/reduce_scatter | solution.py:79
  168.4 52.3 %copy-start.14 = (bf16[128,256]{1,0:T(8,128)(2,1)S(1)}, bf16[128,256]{1,0:T(8,128)(2,1)}, u32[]{:S(2)}) copy-start(bf16[128,256]{1,0:T(8,128)(2,1)} %param.8) | copy-start | bytes 196612
  210.5 47.7 %all-to-all-start.1 = ((bf16[2,768,256]{2,0,1:T(2,128)(2,1)}), bf16[2,768,256]{2,0,1:T(2,128)(2,1)S(1)}, u32[]{:S(2)}, u32[]{:S(2)}) async-start(bf16[2,768,256]{2,0,1:T(2,128)(2,1)} %copy.71), calls=%async_computation.2 | async-start | bytes 1572864 | tf_op jit(solution)/shard_map/all_to_all | solution.py:82
  258.2 17.4 %copy-start.3 = (bf16[2,768,256]{2,0,1:T(2,128)(2,1)}, bf16[2,768,256]{2,0,1:T(2,128)(2,1)S(1)}, u32[]{:S(2)}) copy-start(bf16[2,768,256]{2,0,1:T(2,128)(2,1)S(1)} %all-to-all-done.1) | copy-start | bytes 2359300
  258.2 61.5 %all-to-all-start.2 = ((bf16[2,768,256]{2,0,1:T(2,128)(2,1)}), bf16[2,768,256]{2,0,1:T(2,128)(2,1)}, u32[]{:S(2)}, u32[]{:S(2)}) async-start(bf16[2,768,256]{2,0,1:T(2,128)(2,1)} %copy.74), calls=%async_computation.4 | async-start | bytes 1572864 | tf_op jit(solution)/shard_map/all_to_all | solution.py:83
  275.6 6.7 %copy-start.6 = (bf16[2,768,128]{2,1,0:T(8,128)(2,1)S(1)}, bf16[2,768,128]{2,1,0:T(8,128)(2,1)}, u32[]{:S(2)}) copy-start(bf16[2,768,128]{2,1,0:T(8,128)(2,1)} %copy-done.5) | copy-start | bytes 1179652
  282.3 6.8 %copy-start.4 = (bf16[2,768,256]{2,0,1:T(2,128)(2,1)S(1)}, bf16[2,768,256]{2,0,1:T(2,128)(2,1)}, u32[]{:S(2)}) copy-start(bf16[2,768,256]{2,0,1:T(2,128)(2,1)} %copy-done.3) | copy-start | bytes 2359300
  282.3 10.8 %copy-start.13 = (f32[128,256]{1,0:T(8,128)S(1)}, f32[128,256]{1,0:T(8,128)}, u32[]{:S(2)}) copy-start(f32[128,256]{1,0:T(8,128)} %convert_element_type.91) | copy-start | bytes 393220
  289.1 32.0 %copy-start.12 = (pred[1536,128]{1,0:T(8,128)(4,1)S(1)}, pred[1536,128]{1,0:T(8,128)(4,1)}, u32[]{:S(2)}) copy-start(pred[1536,128]{1,0:T(8,128)(4,1)} %copy-done.11) | copy-start | bytes 589828
  289.1 33.0 %copy-start.1 = (bf16[2,2048,128]{2,1,0:T(8,128)(2,1)S(1)}, bf16[2,2048,128]{2,1,0:T(8,128)(2,1)}, u32[]{:S(2)}) copy-start(bf16[2,2048,128]{2,1,0:T(8,128)(2,1)} %param.11) | copy-start | bytes 3145732
Sparse Core Ops, SparseCore 0:
  78.2 66.7 all-gather.1
  162.2 45.4 reduce-scatter.2
  210.3 44.9 reduce-scatter.4
where the time goes:
time: 329 us
  waiting for transfers between devices  140 us (43%)
  blocking collectives  75.4 us (23%)
  matrix products  46.6 us (14%)
  starting transfers between devices  20.5 us (6%)
  local copies, waits for them, and re-layouts  16.7 us (5%)
  other arithmetic  15.5 us (5%)
  between operations  14.1 us (4%)
    all_gather x1, waiting for transfers between devices, local(): gathered = lax.all_gather(routed, 'et', axis=0)  66.7 us
    all_to_all x1, blocking collectives, local(): lax.all_to_all(routed, 'dp', split_axis=1, concat_axis=2, tiled=True)  50.7 us
    reduce_scatter x1, waiting for transfers between devices, local(): lax.psum_scatter(out_part.astype(jnp.bfloat16), 'et', scatter_dimension=2...  39.3 us
    reduce_scatter x1, waiting for transfers between devices, local(): lax.psum_scatter(in_part.astype(jnp.bfloat16), 'et', scatter_dimension=2,...  33.8 us
    psum x1, blocking collectives, local(): grad_gates = lax.psum(gate_part, 'et')  24.7 us
    all_to_all x1, starting transfers between devices, local(): lax.all_to_all(out_sum, 'dp', split_axis=1, concat_axis=0, tiled=True)  10.1 us
    all_to_all x1, starting transfers between devices, local(): lax.all_to_all(in_sum, 'dp', split_axis=1, concat_axis=0, tiled=True)  10.1 us
    reduce_sum x1, other arithmetic, local(): jnp.sum(jnp.where(match, route_gates.T[None, :, :].astype(jnp.float32), 0...  8.15 us
  transfers between devices with their start and end apart: 5, of which 3 were waited for; matrix products, arithmetic and copies ran while one was open for 12% of the time, Pallas kernels for 0%

commit v1 on v0

--- a/solution.py
+++ b/solution.py
@@ -94,7 +94,11 @@
         back_out[slot_index.reshape(-1)].reshape(tok_rows, per_token, width).astype(jnp.float32)
     )
     gate_part = jnp.sum(cotangent.astype(jnp.float32)[:, None, :] * out_rows, axis=2)
-    grad_gates = lax.psum(gate_part, "et")
+    grad_gates = gate_part
+    for hop in (1, 2, 4):
+        grad_gates = grad_gates + lax.ppermute(
+            grad_gates, "et", [(dev, dev ^ hop) for dev in range(8)]
+        )
     return (mixed, grad_tokens, grad_gates, grad_gate_w, grad_up_w, grad_down)
 
 

time: 329 us -> 314 us (0.954)
  blocking collectives: 75.4 us -> 50.7 us
  waiting for transfers between devices: 140 us -> 148 us
    psum x1 -> x0, blocking collectives: 24.7 us -> none  [local(): grad_gates = lax.psum(gate_part, 'et')]
    ppermute x0 -> x3, waiting for transfers between devices: none -> 7.2 us  [local(): lax.ppermute(grad_gates, 'et', [(dev, dev ^ hop) for dev in range(8)])]
  transfers between devices with their start and end apart: 5 -> 8, of which waited for: 3 -> 5; matrix products, arithmetic and copies ran while one was open for 12% -> 13% of each run, Pallas kernels for 0% -> 0%
where the time goes in v1:
time: 314 us; the launch traced here: 313 us
  waiting for transfers between devices  148 us (47%)
  blocking collectives  50.7 us (16%)
  matrix products  47.7 us (15%)
  starting transfers between devices  21.6 us (7%)
  local copies, waits for them, and re-layouts  15.8 us (5%)
  other arithmetic  15.8 us (5%)
  between operations  14 us (4%)
    all_gather x1, waiting for transfers between devices, local(): gathered = lax.all_gather(routed, 'et', axis=0)  66.7 us
    all_to_all x1, blocking collectives, local(): lax.all_to_all(routed, 'dp', split_axis=1, concat_axis=2, tiled=True)  50.7 us
    reduce_scatter x1, waiting for transfers between devices, local(): lax.psum_scatter(out_part.astype(jnp.bfloat16), 'et', scatter_dimension=2...  39.3 us
    reduce_scatter x1, waiting for transfers between devices, local(): lax.psum_scatter(in_part.astype(jnp.bfloat16), 'et', scatter_dimension=2,...  34.5 us
    all_to_all x1, starting transfers between devices, local(): lax.all_to_all(out_sum, 'dp', split_axis=1, concat_axis=0, tiled=True)  10.1 us
    all_to_all x1, starting transfers between devices, local(): lax.all_to_all(in_sum, 'dp', split_axis=1, concat_axis=0, tiled=True)  10 us
    reduce_sum x1, other arithmetic, local(): jnp.sum(jnp.where(match, route_gates.T[None, :, :].astype(jnp.float32), 0...  8.15 us
    ppermute x3, waiting for transfers between devices, local(): lax.ppermute(grad_gates, 'et', [(dev, dev ^ hop) for dev in range(8)])  7.2 us
  transfers between devices with their start and end apart: 8, of which 5 were waited for; matrix products, arithmetic and copies ran while one was open for 13% of the time, Pallas kernels for 0%

profile of v1, /device:TPU:2, one launch (start us, length us, event | category | flops | bytes accessed | tf_op | source)
XLA Modules:
  0.0 313.4 jit_solution(3871958704486898405)
XLA Ops:
  7.2 0.8 convert_bitcast_fusion
  8.0 0.8 copy.65
  9.6 5.6 %fusion = pred[1536,128]{1,0:T(8,128)(4,1)S(1)} fusion(s32[8,128]{1,0:T(8,128)S(1)} %copy.67), kind=kLoop, calls=%fused_computation.6 | loop fusion | flops 2949120 | bytes 200704 | tf_op jit(solution)/shard_map/reduce_or | solution.py:33
  15.2 8.1 %select_reduce_fusion = bf16[1536,128]{1,0:T(8,128)(2,1)S(1)} fusion(f32[8,128]{1,0:T(8,128)S(1)} %convert_bitcast_fusion, s32[8,128]{1,0:T(8,128)S(1)} %copy.67), kind=kLoop, calls=%fused_computation.4 | loop fusion | flops 4521984 | bytes 401408 | tf_op jit(solution)/shard_map/reduce_sum | solution.py:34
  23.4 1.2 convolution_convert_fusion.1
  24.6 1.3 convolution_convert_fusion.2
  26.1 50.7 %all_to_all.45 = bf16[2,64,24,256]{3,2,0,1:T(8,128)(2,1)S(1)} all-to-all(bf16[2,64,24,256]{3,2,0,1:T(8,128)(2,1)S(1)} %pad_maximum_fusion), channel_id=1, replica_groups=mesh['dp'=32,'et'=8] {'dp'}, dimensions={1} | all-to-all | bytes 3145728 | tf_op jit(solution)/shard_map/all_to_all | solution.py:42
  76.8 1.2 copy.70
  78.3 66.7 %all-gather.2.cloned.1.call-done = bf16[8,2,2,768,256]{4,3,0,2,1:T(8,128)(2,1)} async-done(((bf16[1,2,2,768,256]{4,3,0,2,1:T(8,128)(2,1)}), bf16[8,2,2,768,256]{4,3,0,2,1:T(8,128)(2,1)}) %all-gather.2.cloned.1.call-update) | async-done | bytes 12582928 | tf_op jit(solution)/shard_map/all_gather | solution.py:43
  145.0 4.7 %fusion.9 = f32[2,768,128]{2,1,0:T(8,128)S(1)} fusion(bf16[2,8,256,128]{3,2,1,0:T(8,128)(2,1)S(1)} %bitcast.108, bf16[8,2,2,768,256]{4,3,0,2,1:T(8,128)(2,1)} %all-gather.2.cloned.1.call-done), kind=kOutput, calls=%fused_computation.20 | convolution fusion | flops 805306368 | bytes 8126464 | tf_op jit(solution)/shard_map/jesd,ejdf->esf/dot_general | solution.py:50
  149.7 5.2 %fusion.8 = f32[2,768,128]{2,1,0:T(8,128)S(1)} fusion(bf16[2,8,256,128]{3,2,1,0:T(8,128)(2,1)S(1)} %bitcast.96, bf16[8,2,2,768,256]{4,3,0,2,1:T(8,128)(2,1)} %all-gather.2.cloned.1.call-done), kind=kOutput, calls=%fused_computation.19 | convolution fusion | flops 805306368 | bytes 8126464 | tf_op jit(solution)/shard_map/jesd,ejdf->esf/dot_general | solution.py:49
  154.9 2.0 multiply_convert_fusion
  156.9 4.4 %convolution_convert_fusion = bf16[2,768,2048]{2,1,0:T(8,128)(2,1)} fusion(bf16[2,768,128]{2,1,0:T(8,128)(2,1)S(1)} %get-tuple-element.32, bf16[2,128,2048]{2,1,0:T(8,128)(2,1)S(1)} %copy-done.5), kind=kOutput, calls=%fused_computation.9 | convolution fusion | flops 808452096 | bytes 7733248 | tf_op jit(solution)/shard_map/esf,efd->esd/dot_general | solution.py:54
  161.4 1.8 fusion.24
  163.2 4.4 %add_convert_fusion = bf16[2,768,2048]{2,1,0:T(8,128)(2,1)} fusion(f32[2,768,2048]{2,1,0:T(8,128)S(1)} %fusion.24, bf16[2,768,128]{2,1,0:T(8,128)(2,1)S(1)} %get-tuple-element.30, bf16[2,2048,128]{2,1,0:T(8,128)(2,1)S(1)} %copy-done.4), kind=kOutput, calls=%fused_computation.1 | convolution fusion | flops 811597824 | bytes 20316160 | tf_op jit(solution)/shard_map/esf,edf->esd/dot_general | solution.py:74
  167.7 39.3 %reduce-scatter.3.cloned.1.call-done = bf16[2,768,256]{2,1,0:T(8,128)(2,1)} async-done(((bf16[2,768,2048]{2,1,0:T(8,128)(2,1)}), bf16[2,768,256]{2,1,0:T(8,128)(2,1)}) %reduce-scatter.3.cloned.1.call-update) | async-done | bytes 786448 | tf_op jit(solution)/shard_map/reduce_scatter | solution.py:78
  207.0 2.8 copy.71
  209.8 10.1 %all-to-all-start.1 = ((bf16[2,768,256]{2,0,1:T(2,128)(2,1)}), bf16[2,768,256]{2,0,1:T(2,128)(2,1)S(1)}, u32[]{:S(2)}, u32[]{:S(2)}) async-start(bf16[2,768,256]{2,0,1:T(2,128)(2,1)} %copy.71), calls=%async_computation.2 | async-start | bytes 1572864 | tf_op jit(solution)/shard_map/all_to_all | solution.py:82
  220.1 34.5 %reduce-scatter.5.cloned.1.call-done = bf16[2,768,256]{2,1,0:T(8,128)(2,1)} async-done(((bf16[2,768,2048]{2,1,0:T(8,128)(2,1)}), bf16[2,768,256]{2,1,0:T(8,128)(2,1)}) %reduce-scatter.5.cloned.1.call-update) | async-done | bytes 786448 | tf_op jit(solution)/shard_map/reduce_scatter | solution.py:79
  254.6 2.8 copy.74
  257.4 10.0 %all-to-all-start.2 = ((bf16[2,768,256]{2,0,1:T(2,128)(2,1)}), bf16[2,768,256]{2,0,1:T(2,128)(2,1)S(1)}, u32[]{:S(2)}, u32[]{:S(2)}) async-start(bf16[2,768,256]{2,0,1:T(2,128)(2,1)} %copy.74), calls=%async_computation.4 | async-start | bytes 1572864 | tf_op jit(solution)/shard_map/all_to_all | solution.py:83
  267.5 6.7 %fusion.4 = f32[2,8,256,128]{3,2,1,0:T(8,128)} fusion(bf16[8,2,2,768,256]{4,3,0,2,1:T(8,128)(2,1)} %all-gather.2.cloned.1.call-done, bf16[2,768,128]{2,1,0:T(8,128)(2,1)S(1)} %get-tuple-element.30), kind=kOutput, calls=%fused_computation.12 | convolution fusion | flops 805306368 | bytes 8781824 | tf_op jit(solution)/shard_map/jesd,esf->ejdf/dot_general | solution.py:68
  274.1 6.7 %fusion.5 = f32[2,8,256,128]{3,2,1,0:T(8,128)} fusion(bf16[8,2,2,768,256]{4,3,0,2,1:T(8,128)(2,1)} %all-gather.2.cloned.1.call-done, bf16[2,768,128]{2,1,0:T(8,128)(2,1)S(1)} %get-tuple-element.31), kind=kOutput, calls=%fused_computation.13 | convolution fusion | flops 805306368 | bytes 8781824 | tf_op jit(solution)/shard_map/jesd,esf->ejdf/dot_general | solution.py:65
  280.9 3.9 %gather_fusion = bf16[1024,256]{1,0:T(8,128)(2,1)S(1)} fusion(bf16[1536,256]{1,0:T(8,128)(2,1)S(1)} %bitcast.97, s32[1024]{0:T(1024)S(1)} %broadcast_clamp_fusion), kind=kCustom, calls=%fused_computation | custom fusion | bytes 1052672 | tf_op jit(solution)/shard_map/gather | solution.py:94
  285.2 6.8 %fusion.1 = f32[2,128,8,256]{1,3,2,0:T(8,128)} fusion(bf16[8,2,2,768,256]{4,3,0,2,1:T(8,128)(2,1)} %all-gather.2.cloned.1.call-done, bf16[2,768,128]{2,1,0:T(8,128)(2,1)S(1)} %get-tuple-element.32), kind=kOutput, calls=%fused_computation.7 | convolution fusion | flops 805306368 | bytes 8781824 | tf_op jit(solution)/shard_map/esf,jesd->efjd/dot_general | solution.py:62
  292.0 2.9 copy.82
  294.9 0.8 add.55
  295.8 1.0 convolution_convert_fusion.3
  297.0 3.3 %collective-permute-done.1 = f32[128,8]{1,0:T(8,128)S(1)} collective-permute-done((f32[128,8]{1,0:T(8,128)S(1)}, f32[128,8]{1,0:T(8,128)S(1)}, u32[]{:S(2)}, u32[]{:S(2)}) %collective-permute-start.1) | collective-permute-done | bytes 4128 | tf_op jit(solution)/shard_map/ppermute | solution.py:99
  300.3 0.9 collective-permute-start.2
  301.2 1.1 convolution_convert_fusion.4
  302.3 3.9 %collective-permute-done.2 = f32[128,8]{1,0:T(8,128)S(1)} collective-permute-done((f32[128,8]{1,0:T(8,128)S(1)}, f32[128,8]{1,0:T(8,128)S(1)}, u32[]{:S(2)}, u32[]{:S(2)}) %collective-permute-start.2) | collective-permute-done | bytes 4128 | tf_op jit(solution)/shard_map/ppermute | solution.py:99
  (47 shorter events, 2.9 us)
Async XLA Ops:
  7.2 142.5 %copy-start = (bf16[2,2048,128]{2,1,0:T(8,128)(2,1)S(1)}, bf16[2,2048,128]{2,1,0:T(8,128)(2,1)}, u32[]{:S(2)}) copy-start(bf16[2,2048,128]{2,1,0:T(8,128)(2,1)} %param.11) | copy-start | bytes 3145732
  7.2 137.8 %all-gather.2.cloned.1.call-start = ((), (), s32[]{:S(2)}) async-start(), calls=%async_computation.5 | async-start | bytes 14155776 | tf_op jit(solution)/shard_map/all_gather | solution.py:43
  15.2 10.7 %copy-start.6 = (pred[1536,128]{1,0:T(8,128)(4,1)}, pred[1536,128]{1,0:T(8,128)(4,1)S(1)}, u32[]{:S(2)}) copy-start(pred[1536,128]{1,0:T(8,128)(4,1)S(1)} %fusion) | copy-start | bytes 589828
  24.6 120.4 %copy-start.3 = (bf16[2,2048,128]{2,1,0:T(8,128)(2,1)S(1)}, bf16[2,2048,128]{2,1,0:T(8,128)(2,1)}, u32[]{:S(2)}) copy-start(bf16[2,2048,128]{2,1,0:T(8,128)(2,1)} %param.12) | copy-start | bytes 3145732
  78.0 128.9 %reduce-scatter.3.cloned.1.call-start = ((), (), s32[]{:S(2)}) async-start(), calls=%async_computation.6 | async-start | bytes 7077888 | tf_op jit(solution)/shard_map/reduce_scatter | solution.py:78
  144.9 10.0 %copy-start.2 = (bf16[8,2,2,768,256]{4,3,0,2,1:T(8,128)(2,1)S(1)}, bf16[8,2,2,768,256]{4,3,0,2,1:T(8,128)(2,1)}, u32[]{:S(2)}) copy-start(bf16[8,2,2,768,256]{4,3,0,2,1:T(8,128)(2,1)} %all-gather.2.cloned.1.call-done) | copy-start | bytes 37748740
  149.7 5.3 %copy-start.5 = (bf16[2,128,2048]{2,1,0:T(8,128)(2,1)S(1)}, bf16[2,128,2048]{2,1,0:T(8,128)(2,1)}, u32[]{:S(2)}) copy-start(bf16[2,128,2048]{2,1,0:T(8,128)(2,1)} %param.13) | copy-start | bytes 3145732
  161.4 93.3 %reduce-scatter.5.cloned.1.call-start = ((), (), s32[]{:S(2)}) async-start(), calls=%async_computation.7 | async-start | bytes 7077888 | tf_op jit(solution)/shard_map/reduce_scatter | solution.py:79
  161.4 1.8 copy-start.4
  167.7 52.3 %copy-start.8 = (bf16[128,256]{1,0:T(8,128)(2,1)S(1)}, bf16[128,256]{1,0:T(8,128)(2,1)}, u32[]{:S(2)}) copy-start(bf16[128,256]{1,0:T(8,128)(2,1)} %param.8) | copy-start | bytes 196612
  209.8 47.6 %all-to-all-start.1 = ((bf16[2,768,256]{2,0,1:T(2,128)(2,1)}), bf16[2,768,256]{2,0,1:T(2,128)(2,1)S(1)}, u32[]{:S(2)}, u32[]{:S(2)}) async-start(bf16[2,768,256]{2,0,1:T(2,128)(2,1)} %copy.71), calls=%async_computation.2 | async-start | bytes 1572864 | tf_op jit(solution)/shard_map/all_to_all | solution.py:82
  257.4 39.4 %all-to-all-start.2 = ((bf16[2,768,256]{2,0,1:T(2,128)(2,1)}), bf16[2,768,256]{2,0,1:T(2,128)(2,1)S(1)}, u32[]{:S(2)}, u32[]{:S(2)}) async-start(bf16[2,768,256]{2,0,1:T(2,128)(2,1)} %copy.74), calls=%async_computation.4 | async-start | bytes 1572864 | tf_op jit(solution)/shard_map/all_to_all | solution.py:83
  285.1 9.8 %collective-permute-start = (f32[128,8]{1,0:T(8,128)S(1)}, f32[128,8]{1,0:T(8,128)}, u32[]{:S(2)}, u32[]{:S(2)}) collective-permute-start(f32[128,8]{1,0:T(8,128)S(1)} %fusion.15), channel_id=1, source_target_pairs={{0,1},{1,0},{2,3},{3,2},{4,5},{5,4},{6,7},{7,6},{8,9},{9,8},{10,11... | collective-permute-start | bytes 12296 | tf_op jit(solution)/shard_map/ppermute | solution.py:99
  285.2 21.7 %copy-start.1 = (bf16[2,2048,128]{2,1,0:T(8,128)(2,1)S(1)}, bf16[2,2048,128]{2,1,0:T(8,128)(2,1)}, u32[]{:S(2)}) copy-start(bf16[2,2048,128]{2,1,0:T(8,128)(2,1)} %param.11) | copy-start | bytes 3145732
  292.0 9.3 %copy-start.7 = (pred[1536,128]{1,0:T(8,128)(4,1)S(1)}, pred[1536,128]{1,0:T(8,128)(4,1)}, u32[]{:S(2)}) copy-start(pred[1536,128]{1,0:T(8,128)(4,1)} %copy-done.6) | copy-start | bytes 589828
  295.7 4.6 %collective-permute-start.1 = (f32[128,8]{1,0:T(8,128)S(1)}, f32[128,8]{1,0:T(8,128)S(1)}, u32[]{:S(2)}, u32[]{:S(2)}) collective-permute-start(f32[128,8]{1,0:T(8,128)S(1)} %add.55), channel_id=1, source_target_pairs={{0,2},{1,3},{2,0},{3,1},{4,6},{5,7},{6,4},{7,5},{8,10},{9,11},{10,... | collective-permute-start | bytes 12296 | tf_op jit(solution)/shard_map/ppermute | solution.py:99
  300.3 5.9 %collective-permute-start.2 = (f32[128,8]{1,0:T(8,128)S(1)}, f32[128,8]{1,0:T(8,128)S(1)}, u32[]{:S(2)}, u32[]{:S(2)}) collective-permute-start(f32[128,8]{1,0:T(8,128)S(1)} %add.56), channel_id=1, source_target_pairs={{0,4},{1,5},{2,6},{3,7},{4,0},{5,1},{6,2},{7,3},{8,12},{9,13},{10,... | collective-permute-start | bytes 12296 | tf_op jit(solution)/shard_map/ppermute | solution.py:99
Sparse Core Ops, SparseCore 0:
  78.2 66.7 all-gather.1
  161.5 45.4 reduce-scatter.2
  209.5 45.0 reduce-scatter.4
